TPU v7x, 32 devices: a whole 2x2x4 slice. The times are simulated.
32 devices in a mesh: area: 4 (over x, core), sub: 8 (over z, y).
Axes of the slice: x: 2, y: 2, z: 4, core: 2. Of those that a mesh axis runs over, the one named last changes fastest.
Arguments:
- blocks: float32 [4, 512, 64, 256], P('area', 'sub'), as said below
- pattern: int32 [4, 512, 4], P('area', 'sub'), may hold values from 0 to 511, as said below
- line_ends: int32 [4, 2, 64], P('area'), may hold values from 0 to 32767, as said below
- sources: float32 [4, 4, 32768], P(None, 'area', 'sub'), may hold values from -6 to 6
- capacity: float32 [4, 32768], P('area', 'sub'), may hold values from 0.2 to 2
- start_volt: float32 [4, 32768], P('area', 'sub'), may hold values from -6 to 6
- start_hist: float32 [4, 2, 64], P('area'), may hold values from -6 to 6
- surge: float32 [4, 64], P('area'), may hold values from 0.2 to 1
Outputs:
- volt: float32 [4, 32768], P('area', 'sub')
- hist: float32 [4, 2, 64], P('area')
Inputs may be any that keep to these rules, and one draw needn't show every extreme that they name: pattern[a, r, 0] = r. Split the 512 block rows of an area into aligned groups of 64: the other entries of a row never point into the row's own group, no two of them in one group are equal, and the entries of one group point into between 27 and 28 distinct block rows of each other group, exactly 28 for some group. `line_ends`: within an area the line-end buses are distinct and rise from the first left end to the last right end. `blocks`: the diagonal of each first stored block lies in 2 to 4.
All inputs are finite; a program needn't handle non-finite values.
Results may differ from a plain program's by a relative error of at most 0.00011.
Values sent between devices are 32-bit elements; how exact they have to be, the bound alone decides.
No kernel may reach another device: no remote copies, remote signals or barrier semaphores. Data moves between devices by JAX's collectives and lax.ppermute only.
A program may use at most 64 MiB of HBM per device.

v0:
```python
import jax
import jax.numpy as jnp
from jax import lax
from jax.sharding import PartitionSpec as P

STEPS = 4
SWEEPS = 8


def shifted(value, axis, steps):
    count = lax.axis_size(axis)
    pairs = [(source, (source + steps) % count) for source in range(count)]
    return lax.ppermute(value, axis, pairs)


def collect(field):
    return lax.all_gather(field, "sub", axis=1, tiled=True)


def apply_blocks(blocks, own_part, others):
    picked = jnp.concatenate([own_part, others], axis=1)
    result = jnp.einsum("rik,rk->ri", blocks[0], picked, precision=lax.Precision.HIGHEST)
    return result.reshape(1, -1)


def on_device(blocks, pattern, line_ends, sources, capacity, start_volt, start_hist, surge):
    width = blocks.shape[2]
    rows_here = blocks.shape[1]
    local_count = rows_here * width
    offset = lax.axis_index("sub") * local_count
    diag = jnp.diagonal(blocks[..., :width], axis1=2, axis2=3).reshape(1, local_count)
    system_diag = diag + capacity
    remote_cols = pattern[0][:, 1:].reshape(-1)
    local_ends = line_ends - offset
    inside = (local_ends >= 0) & (local_ends < local_count)
    safe_ends = jnp.clip(local_ends, 0, local_count - 1)
    volt = start_volt
    hist = start_hist
    carried = []
    for step in range(STEPS):
        rhs = sources[step] + capacity * volt
        inject = jnp.where(inside, -hist, 0.0)
        rhs = rhs.at[0, safe_ends.reshape(-1)].add(inject.reshape(-1))
        field = volt
        for sweep in range(SWEEPS):
            own_part = field.reshape(rows_here, width)
            whole = collect(field)
            others = whole.reshape(-1, width)[remote_cols]
            others = others.reshape(rows_here, -1)
            result = apply_blocks(blocks, own_part, others)
            field = field + (rhs - result - capacity * field) / system_diag
        volt = field
        partial_volt = jnp.where(inside, volt[0][safe_ends[0]][None], 0.0)
        end_volt = lax.psum(partial_volt, "sub")
        message = -2.0 * surge * end_volt[:, 1] - hist[:, 1]
        new_left = shifted(message, "area", 1)
        outgoing_ends = jnp.stack([end_volt[:, 0], hist[:, 0]], axis=1)
        from_right = shifted(outgoing_ends, "area", -1)
        new_right = -2.0 * surge * from_right[:, 0] - from_right[:, 1]
        hist = jnp.stack([new_left, new_right], axis=1)
    return (volt, hist)


def solution(mesh):
    in_specs = (
        P("area", "sub", None, None),
        P("area", "sub", None),
        P("area", None, None),
        P(None, "area", "sub"),
        P("area", "sub"),
        P("area", "sub"),
        P("area", None, None),
        P("area", None),
    )
    out_specs = (P("area", "sub"), P("area", None, None))
    return jax.shard_map(
        on_device, mesh=mesh, in_specs=in_specs, out_specs=out_specs, check_vma=False
    )
```

profile of v0, /device:TPU:0, one launch (start us, length us, event | category | flops | bytes accessed | tf_op | source)
XLA Modules:
  0.0 1362.5 jit_solution(36075500390137617)
XLA Ops:
  2.0 32.5 %all_gather.96 = f32[1,32768]{1,0:T(1,128)S(1)} all-gather(f32[1,4096]{1,0:T(1,128)} %param.13), channel_id=1, replica_groups=mesh['area'=4,'sub'=8] {'sub'}, dimensions={1}, use_global_device_ids=true | all-gather | bytes 147456 | tf_op jit(solution)/shard_map/all_gather | solution.py:17
  51.7 30.5 %all_gather.97 = f32[1,32768]{1,0:T(1,128)S(1)} all-gather(f32[1,4096]{1,0:T(1,128)S(1)} %get-tuple-element.71), channel_id=1, replica_groups=mesh['area'=4,'sub'=8] {'sub'}, dimensions={1}, use_global_device_ids=true | all-gather | bytes 147456 | tf_op jit(solution)/shard_map/all_gather | solution.py:17
  84.2 5.7 fusion.60
  90.7 30.7 %all_gather.98 = f32[1,32768]{1,0:T(1,128)S(1)} all-gather(f32[1,4096]{1,0:T(1,128)S(1)} %get-tuple-element.69), channel_id=1, replica_groups=mesh['area'=4,'sub'=8] {'sub'}, dimensions={1}, use_global_device_ids=true | all-gather | bytes 147456 | tf_op jit(solution)/shard_map/all_gather | solution.py:17
  123.5 5.7 fusion.58
  130.0 30.5 %all_gather.99 = f32[1,32768]{1,0:T(1,128)S(1)} all-gather(f32[1,4096]{1,0:T(1,128)S(1)} %get-tuple-element.67), channel_id=1, replica_groups=mesh['area'=4,'sub'=8] {'sub'}, dimensions={1}, use_global_device_ids=true | all-gather | bytes 147456 | tf_op jit(solution)/shard_map/all_gather | solution.py:17
  162.5 5.7 fusion.56
  169.1 30.5 %all_gather.100 = f32[1,32768]{1,0:T(1,128)S(1)} all-gather(f32[1,4096]{1,0:T(1,128)S(1)} %get-tuple-element.65), channel_id=1, replica_groups=mesh['area'=4,'sub'=8] {'sub'}, dimensions={1}, use_global_device_ids=true | all-gather | bytes 147456 | tf_op jit(solution)/shard_map/all_gather | solution.py:17
  201.6 5.7 fusion.54
  208.2 30.9 %all_gather.101 = f32[1,32768]{1,0:T(1,128)S(1)} all-gather(f32[1,4096]{1,0:T(1,128)S(1)} %get-tuple-element.63), channel_id=1, replica_groups=mesh['area'=4,'sub'=8] {'sub'}, dimensions={1}, use_global_device_ids=true | all-gather | bytes 147456 | tf_op jit(solution)/shard_map/all_gather | solution.py:17
  241.1 5.7 fusion.52
  247.7 30.5 %all_gather.102 = f32[1,32768]{1,0:T(1,128)S(1)} all-gather(f32[1,4096]{1,0:T(1,128)S(1)} %get-tuple-element.61), channel_id=1, replica_groups=mesh['area'=4,'sub'=8] {'sub'}, dimensions={1}, use_global_device_ids=true | all-gather | bytes 147456 | tf_op jit(solution)/shard_map/all_gather | solution.py:17
  280.2 5.7 fusion.50
  286.7 30.5 %all_gather.103 = f32[1,32768]{1,0:T(1,128)S(1)} all-gather(f32[1,4096]{1,0:T(1,128)S(1)} %get-tuple-element.59), channel_id=1, replica_groups=mesh['area'=4,'sub'=8] {'sub'}, dimensions={1}, use_global_device_ids=true | all-gather | bytes 147456 | tf_op jit(solution)/shard_map/all_gather | solution.py:17
  319.3 5.7 fusion.48
  327.2 21.3 %psum.28 = f32[1,2,64]{2,1,0:T(2,128)S(1)} all-reduce(f32[1,2,64]{2,1,0:T(2,128)S(1)} %broadcast_select_fusion.3), channel_id=1, replica_groups=mesh['area'=4,'sub'=8] {'sub'}, use_global_device_ids=true, to_apply=%region_1.2 | all-reduce | flops 128 | bytes 1024 | tf_op jit(solution)/shard_map/psum | solution.py:54
  348.8 30.5 %all_gather.104 = f32[1,32768]{1,0:T(1,128)S(1)} all-gather(f32[1,4096]{1,0:T(1,128)S(1)} %get-tuple-element.53), channel_id=1, replica_groups=mesh['area'=4,'sub'=8] {'sub'}, dimensions={1}, use_global_device_ids=true | all-gather | bytes 147456 | tf_op jit(solution)/shard_map/all_gather | solution.py:17
  381.4 5.7 fusion.46
  389.5 30.5 %all_gather.105 = f32[1,32768]{1,0:T(1,128)S(1)} all-gather(f32[1,4096]{1,0:T(1,128)S(1)} %get-tuple-element.51), channel_id=1, replica_groups=mesh['area'=4,'sub'=8] {'sub'}, dimensions={1}, use_global_device_ids=true | all-gather | bytes 147456 | tf_op jit(solution)/shard_map/all_gather | solution.py:17
  422.2 5.7 fusion.44
  428.7 30.7 %all_gather.106 = f32[1,32768]{1,0:T(1,128)S(1)} all-gather(f32[1,4096]{1,0:T(1,128)S(1)} %get-tuple-element.49), channel_id=1, replica_groups=mesh['area'=4,'sub'=8] {'sub'}, dimensions={1}, use_global_device_ids=true | all-gather | bytes 147456 | tf_op jit(solution)/shard_map/all_gather | solution.py:17
  461.6 5.7 fusion.42
  468.2 30.6 %all_gather.107 = f32[1,32768]{1,0:T(1,128)S(1)} all-gather(f32[1,4096]{1,0:T(1,128)S(1)} %get-tuple-element.47), channel_id=1, replica_groups=mesh['area'=4,'sub'=8] {'sub'}, dimensions={1}, use_global_device_ids=true | all-gather | bytes 147456 | tf_op jit(solution)/shard_map/all_gather | solution.py:17
  500.9 5.7 fusion.40
  507.4 30.6 %all_gather.108 = f32[1,32768]{1,0:T(1,128)S(1)} all-gather(f32[1,4096]{1,0:T(1,128)S(1)} %get-tuple-element.45), channel_id=1, replica_groups=mesh['area'=4,'sub'=8] {'sub'}, dimensions={1}, use_global_device_ids=true | all-gather | bytes 147456 | tf_op jit(solution)/shard_map/all_gather | solution.py:17
  540.1 5.7 fusion.38
  546.7 30.9 %all_gather.109 = f32[1,32768]{1,0:T(1,128)S(1)} all-gather(f32[1,4096]{1,0:T(1,128)S(1)} %get-tuple-element.43), channel_id=1, replica_groups=mesh['area'=4,'sub'=8] {'sub'}, dimensions={1}, use_global_device_ids=true | all-gather | bytes 147456 | tf_op jit(solution)/shard_map/all_gather | solution.py:17
  579.8 5.7 fusion.36
  586.3 30.5 %all_gather.110 = f32[1,32768]{1,0:T(1,128)S(1)} all-gather(f32[1,4096]{1,0:T(1,128)S(1)} %get-tuple-element.41), channel_id=1, replica_groups=mesh['area'=4,'sub'=8] {'sub'}, dimensions={1}, use_global_device_ids=true | all-gather | bytes 147456 | tf_op jit(solution)/shard_map/all_gather | solution.py:17
  619.0 5.7 fusion.34
  625.5 30.5 %all_gather.111 = f32[1,32768]{1,0:T(1,128)S(1)} all-gather(f32[1,4096]{1,0:T(1,128)S(1)} %get-tuple-element.39), channel_id=1, replica_groups=mesh['area'=4,'sub'=8] {'sub'}, dimensions={1}, use_global_device_ids=true | all-gather | bytes 147456 | tf_op jit(solution)/shard_map/all_gather | solution.py:17
  658.2 5.7 fusion.32
  664.7 30.7 %all_gather.112 = f32[1,32768]{1,0:T(1,128)S(1)} all-gather(f32[1,4096]{1,0:T(1,128)S(1)} %get-tuple-element.35), channel_id=1, replica_groups=mesh['area'=4,'sub'=8] {'sub'}, dimensions={1}, use_global_device_ids=true | all-gather | bytes 147456 | tf_op jit(solution)/shard_map/all_gather | solution.py:17
  698.6 17.1 %psum.29 = f32[1,2,64]{2,1,0:T(2,128)S(1)} all-reduce(f32[1,2,64]{2,1,0:T(2,128)S(1)} %broadcast_select_fusion.2), channel_id=1, replica_groups=mesh['area'=4,'sub'=8] {'sub'}, use_global_device_ids=true, to_apply=%region_3.4 | all-reduce | flops 128 | bytes 1024 | tf_op jit(solution)/shard_map/psum | solution.py:54
  726.8 30.6 %all_gather.113 = f32[1,32768]{1,0:T(1,128)S(1)} all-gather(f32[1,4096]{1,0:T(1,128)S(1)} %get-tuple-element.33), channel_id=1, replica_groups=mesh['area'=4,'sub'=8] {'sub'}, dimensions={1}, use_global_device_ids=true | all-gather | bytes 147456 | tf_op jit(solution)/shard_map/all_gather | solution.py:17
  759.6 5.7 fusion.28
  766.1 30.7 %all_gather.114 = f32[1,32768]{1,0:T(1,128)S(1)} all-gather(f32[1,4096]{1,0:T(1,128)S(1)} %get-tuple-element.31), channel_id=1, replica_groups=mesh['area'=4,'sub'=8] {'sub'}, dimensions={1}, use_global_device_ids=true | all-gather | bytes 147456 | tf_op jit(solution)/shard_map/all_gather | solution.py:17
  799.0 5.7 fusion.26
  805.5 30.5 %all_gather.115 = f32[1,32768]{1,0:T(1,128)S(1)} all-gather(f32[1,4096]{1,0:T(1,128)S(1)} %get-tuple-element.29), channel_id=1, replica_groups=mesh['area'=4,'sub'=8] {'sub'}, dimensions={1}, use_global_device_ids=true | all-gather | bytes 147456 | tf_op jit(solution)/shard_map/all_gather | solution.py:17
  838.2 5.7 fusion.24
  844.7 30.6 %all_gather.116 = f32[1,32768]{1,0:T(1,128)S(1)} all-gather(f32[1,4096]{1,0:T(1,128)S(1)} %get-tuple-element.27), channel_id=1, replica_groups=mesh['area'=4,'sub'=8] {'sub'}, dimensions={1}, use_global_device_ids=true | all-gather | bytes 147456 | tf_op jit(solution)/shard_map/all_gather | solution.py:17
  877.5 5.7 fusion.22
  884.0 30.9 %all_gather.117 = f32[1,32768]{1,0:T(1,128)S(1)} all-gather(f32[1,4096]{1,0:T(1,128)S(1)} %get-tuple-element.25), channel_id=1, replica_groups=mesh['area'=4,'sub'=8] {'sub'}, dimensions={1}, use_global_device_ids=true | all-gather | bytes 147456 | tf_op jit(solution)/shard_map/all_gather | solution.py:17
  917.1 5.7 fusion.20
  923.6 30.5 %all_gather.118 = f32[1,32768]{1,0:T(1,128)S(1)} all-gather(f32[1,4096]{1,0:T(1,128)S(1)} %get-tuple-element.23), channel_id=1, replica_groups=mesh['area'=4,'sub'=8] {'sub'}, dimensions={1}, use_global_device_ids=true | all-gather | bytes 147456 | tf_op jit(solution)/shard_map/all_gather | solution.py:17
  956.3 5.7 fusion.18
  962.9 30.5 %all_gather.119 = f32[1,32768]{1,0:T(1,128)S(1)} all-gather(f32[1,4096]{1,0:T(1,128)S(1)} %get-tuple-element.21), channel_id=1, replica_groups=mesh['area'=4,'sub'=8] {'sub'}, dimensions={1}, use_global_device_ids=true | all-gather | bytes 147456 | tf_op jit(solution)/shard_map/all_gather | solution.py:17
  995.5 5.7 fusion.16
  1002.1 30.7 %all_gather.120 = f32[1,32768]{1,0:T(1,128)S(1)} all-gather(f32[1,4096]{1,0:T(1,128)S(1)} %get-tuple-element.17), channel_id=1, replica_groups=mesh['area'=4,'sub'=8] {'sub'}, dimensions={1}, use_global_device_ids=true | all-gather | bytes 147456 | tf_op jit(solution)/shard_map/all_gather | solution.py:17
  1035.9 19.4 %psum.30 = f32[1,2,64]{2,1,0:T(2,128)S(1)} all-reduce(f32[1,2,64]{2,1,0:T(2,128)S(1)} %broadcast_select_fusion.1), channel_id=1, replica_groups=mesh['area'=4,'sub'=8] {'sub'}, use_global_device_ids=true, to_apply=%region_5.6 | all-reduce | flops 128 | bytes 1024 | tf_op jit(solution)/shard_map/psum | solution.py:54
  1065.2 30.6 %all_gather.121 = f32[1,32768]{1,0:T(1,128)S(1)} all-gather(f32[1,4096]{1,0:T(1,128)S(1)} %get-tuple-element.15), channel_id=1, replica_groups=mesh['area'=4,'sub'=8] {'sub'}, dimensions={1}, use_global_device_ids=true | all-gather | bytes 147456 | tf_op jit(solution)/shard_map/all_gather | solution.py:17
  1097.8 5.7 fusion.12
  1104.3 30.8 %all_gather.122 = f32[1,32768]{1,0:T(1,128)S(1)} all-gather(f32[1,4096]{1,0:T(1,128)S(1)} %get-tuple-element.13), channel_id=1, replica_groups=mesh['area'=4,'sub'=8] {'sub'}, dimensions={1}, use_global_device_ids=true | all-gather | bytes 147456 | tf_op jit(solution)/shard_map/all_gather | solution.py:17
  1137.1 5.7 fusion.10
  1143.6 30.6 %all_gather.123 = f32[1,32768]{1,0:T(1,128)S(1)} all-gather(f32[1,4096]{1,0:T(1,128)S(1)} %get-tuple-element.11), channel_id=1, replica_groups=mesh['area'=4,'sub'=8] {'sub'}, dimensions={1}, use_global_device_ids=true | all-gather | bytes 147456 | tf_op jit(solution)/shard_map/all_gather | solution.py:17
  1176.2 5.7 fusion.8
  1182.8 30.6 %all_gather.124 = f32[1,32768]{1,0:T(1,128)S(1)} all-gather(f32[1,4096]{1,0:T(1,128)S(1)} %get-tuple-element.9), channel_id=1, replica_groups=mesh['area'=4,'sub'=8] {'sub'}, dimensions={1}, use_global_device_ids=true | all-gather | bytes 147456 | tf_op jit(solution)/shard_map/all_gather | solution.py:17
  1215.4 5.7 fusion.6
  1221.9 30.8 %all_gather.125 = f32[1,32768]{1,0:T(1,128)S(1)} all-gather(f32[1,4096]{1,0:T(1,128)S(1)} %get-tuple-element.7), channel_id=1, replica_groups=mesh['area'=4,'sub'=8] {'sub'}, dimensions={1}, use_global_device_ids=true | all-gather | bytes 147456 | tf_op jit(solution)/shard_map/all_gather | solution.py:17
  1254.7 5.7 fusion.4
  1261.3 30.5 %all_gather.126 = f32[1,32768]{1,0:T(1,128)S(1)} all-gather(f32[1,4096]{1,0:T(1,128)S(1)} %get-tuple-element.5), channel_id=1, replica_groups=mesh['area'=4,'sub'=8] {'sub'}, dimensions={1}, use_global_device_ids=true | all-gather | bytes 147456 | tf_op jit(solution)/shard_map/all_gather | solution.py:17
  1293.8 5.7 fusion.2
  1300.3 30.5 %all_gather.127 = f32[1,32768]{1,0:T(1,128)S(1)} all-gather(f32[1,4096]{1,0:T(1,128)S(1)} %get-tuple-element.3), channel_id=1, replica_groups=mesh['area'=4,'sub'=8] {'sub'}, dimensions={1}, use_global_device_ids=true | all-gather | bytes 147456 | tf_op jit(solution)/shard_map/all_gather | solution.py:17
  1340.0 17.1 %psum.31 = f32[1,2,64]{2,1,0:T(2,128)S(1)} all-reduce(f32[1,2,64]{2,1,0:T(2,128)S(1)} %broadcast_select_fusion), channel_id=1, replica_groups=mesh['area'=4,'sub'=8] {'sub'}, use_global_device_ids=true, to_apply=%region_7.8 | all-reduce | flops 128 | bytes 1024 | tf_op jit(solution)/shard_map/psum | solution.py:54
  (355 shorter events, 142.7 us)
Async XLA Ops:
  37.1 343.3 %copy-start.3 = (s32[1024]{0:T(1024)}, s32[1024]{0:T(1024)S(1)}, u32[]{:S(2)}) copy-start(s32[1024]{0:T(1024)S(1)} %pad_clamp_fusion.1) | copy-start | bytes 12292
  39.4 2.2 copy-start
  39.4 6.1 slice-start
  41.6 9.3 copy-start.2
  41.6 9.3 copy-start.5
  285.9 62.6 %slice-start.1 = ((f32[1,2,64]{2,1,0:T(2,128)}), f32[1,1,64]{2,1,0:T(1,128)S(1)}, s32[]{:S(2)}) async-start(f32[1,2,64]{2,1,0:T(2,128)} %param.14), calls=%async_computation.1 | async-start | bytes 1024 | tf_op jit(solution)/shard_map/slice | solution.py:57
  285.9 93.4 %copy-start.6 = (f32[4,1,4096]{2,1,0:T(1,128)S(1)}, f32[4,1,4096]{2,1,0:T(1,128)}, u32[]{:S(2)}) copy-start(f32[4,1,4096]{2,1,0:T(1,128)} %param.11) | copy-start | bytes 196612
  319.0 62.3 %copy-start.7 = (f32[1,64]{1,0:T(1,128)S(1)}, f32[1,64]{1,0:T(1,128)}, u32[]{:S(2)}) copy-start(f32[1,64]{1,0:T(1,128)} %param.15) | copy-start | bytes 772
  319.0 62.3 %copy-start.8 = (f32[1,2,64]{2,1,0:T(2,128)S(1)}, f32[1,2,64]{2,1,0:T(2,128)}, u32[]{:S(2)}) copy-start(f32[1,2,64]{2,1,0:T(2,128)} %param.14) | copy-start | bytes 1540
  348.5 32.8 %collective-permute-start.1 = (f32[1,2,64]{2,1,0:T(2,128)S(1)}, f32[1,2,64]{2,1,0:T(2,128)S(1)}, u32[]{:S(2)}, u32[]{:S(2)}) collective-permute-start(f32[1,2,64]{2,1,0:T(2,128)S(1)} %pad_maximum_fusion), channel_id=1, source_target_pairs={{0,24},{8,0},{16,8},{24,16},{1,25},{9,1},{17,9},{25,17},{2,26},{10... | collective-permute-start | bytes 1544 | tf_op jit(solution)/shard_map/ppermute | solution.py:13
  381.4 5.9 collective-permute-start
  624.7 71.8 %copy-start.4 = (s32[1024]{0:T(1024)S(1)}, s32[1024]{0:T(1024)}, u32[]{:S(2)}) copy-start(s32[1024]{0:T(1024)} %copy-done.3) | copy-start | bytes 12292
  715.8 1.4 collective-permute-start.3
  717.1 7.4 collective-permute-start.2
  1055.4 1.4 collective-permute-start.5
  1056.8 6.2 collective-permute-start.4
  1338.7 23.3 %copy-start.1 = (f32[1,4096]{1,0:T(1,128)}, f32[1,4096]{1,0:T(1,128)S(1)}, u32[]{:S(2)}) copy-start(f32[1,4096]{1,0:T(1,128)S(1)} %divide_add_fusion) | copy-start | bytes 49156
  1357.1 1.4 collective-permute-start.7
  1358.5 3.0 collective-permute-start.6
where the time goes:
time: 1370 us; the launch traced here: 1360 us
  blocking collectives  1060 us (77%)
  matrix products  181 us (13%)
  other arithmetic  64.7 us (5%)
  local copies, waits for them, and re-layouts  48.1 us (4%)
    all_gather x32, blocking collectives, collect(): return lax.all_gather(field, 'sub', axis=1, tiled=True)  982 us
    dot_general x32, matrix products, apply_blocks(): jnp.einsum('rik,rk->ri', blocks[0], picked, precision=lax.Precision.HIGHEST)  181 us
    psum x4, blocking collectives, on_device(): end_volt = lax.psum(partial_volt, 'sub')  75 us
    all_gather x32, other arithmetic, collect(): return lax.all_gather(field, 'sub', axis=1, tiled=True)  30.4 us
  transfers between devices with their start and end apart: 8, of which 4 were waited for; matrix products, arithmetic and copies ran while one was open for 1% of the time, Pallas kernels for 0%

commit v1 on v0

--- a/solution.py
+++ b/solution.py
@@ -7,6 +7,27 @@
 SWEEPS = 8
 
 
+def collect_2(x, axis, dim):
+    size, index, span = (lax.axis_size(axis), lax.axis_index(axis), x.shape[dim])
+    forward = [(i, (i + 1) % size) for i in range(size)]
+    downward = [(i, (i - 1) % size) for i in range(size)]
+    whole = jnp.zeros((*x.shape[:dim], size * span, *x.shape[dim + 1 :]), x.dtype)
+    whole = lax.dynamic_update_slice_in_dim(whole, x, index * span, axis=dim)
+    from_left = from_right = x
+    middle = size // 2
+    for step in range(1, middle + 1):
+        from_left = lax.ppermute(from_left, axis, forward)
+        whole = lax.dynamic_update_slice_in_dim(
+            whole, from_left, (index - step) % size * span, axis=dim
+        )
+        if step < size - middle:
+            from_right = lax.ppermute(from_right, axis, downward)
+            whole = lax.dynamic_update_slice_in_dim(
+                whole, from_right, (index + step) % size * span, axis=dim
+            )
+    return whole
+
+
 def shifted(value, axis, steps):
     count = lax.axis_size(axis)
     pairs = [(source, (source + steps) % count) for source in range(count)]
@@ -14,7 +35,7 @@
 
 
 def collect(field):
-    return lax.all_gather(field, "sub", axis=1, tiled=True)
+    return collect_2(field, "sub", 1)
 
 
 def apply_blocks(blocks, own_part, others):

time: 1370 us -> 1230 us (0.90)
  blocking collectives: 1060 us -> 68.4 us
  starting transfers between devices: 4.31 us -> 462 us
  waiting for transfers between devices: 4.78 us -> 306 us
  local copies, waits for them, and re-layouts: 48.1 us -> 120 us
    all_gather x32 -> x0, blocking collectives: 982 us -> none  [collect(): return lax.all_gather(field, 'sub', axis=1, tiled=True)]
    ppermute x0 -> x224, starting transfers between devices: none -> 461 us  [the longest x96 446 us: collect_2(): from_right = lax.ppermute(from_right, axis, downward)]
    ppermute x0 -> x224, waiting for transfers between devices: none -> 295 us  [the longest x128 295 us: collect_2(): from_left = lax.ppermute(from_left, axis, forward)]
    dynamic_update_slice x0 -> x253, local copies, waits for them, and re-layouts: none -> 64.5 us  [the longest x129 32.5 us: collect_2(): lax.dynamic_update_slice_in_dim(whole, from_left, (index - step) % size *...]
    dynamic_update_slice x0 -> x32, other arithmetic: none -> 42.2 us  [collect_2(): lax.dynamic_update_slice_in_dim(whole, from_left, (index - step) % size *...]
    all_gather x32 -> x0, other arithmetic: 30.4 us -> none  [collect(): return lax.all_gather(field, 'sub', axis=1, tiled=True)]
  transfers between devices with their start and end apart: 8 -> 232, of which waited for: 4 -> 129; matrix products, arithmetic and copies ran while one was open for 1% -> 7% of each run, Pallas kernels for 0% -> 0%
where the time goes in v1:
time: 1230 us; the launch traced here: 1220 us
  starting transfers between devices  462 us (38%)
  waiting for transfers between devices  306 us (25%)
  matrix products  183 us (15%)
  local copies, waits for them, and re-layouts  120 us (10%)
  other arithmetic  76.6 us (6%)
  blocking collectives  68.4 us (6%)
    ppermute x96, starting transfers between devices, collect_2(): from_right = lax.ppermute(from_right, axis, downward)  446 us
    ppermute x128, waiting for transfers between devices, collect_2(): from_left = lax.ppermute(from_left, axis, forward)  295 us
    dot_general x32, matrix products, apply_blocks(): jnp.einsum('rik,rk->ri', blocks[0], picked, precision=lax.Precision.HIGHEST)  183 us
    psum x4, blocking collectives, on_device(): end_volt = lax.psum(partial_volt, 'sub')  68.4 us
    dynamic_update_slice x32, other arithmetic, collect_2(): lax.dynamic_update_slice_in_dim(whole, from_left, (index - step) % size *...  42.2 us
    dynamic_update_slice x129, local copies, waits for them, and re-layouts, collect_2(): lax.dynamic_update_slice_in_dim(whole, from_left, (index - step) % size *...  32.5 us
  transfers between devices with their start and end apart: 232, of which 129 were waited for; matrix products, arithmetic and copies ran while one was open for 7% of the time, Pallas kernels for 0%

profile of v1, /device:TPU:0, one launch (start us, length us, event | category | flops | bytes accessed | tf_op | source)
XLA Modules:
  0.0 1220.7 jit_solution(8632390136626675780)
XLA Ops:
  30.0 6.4 collective-permute-done.6
  38.4 5.7 fusion.62
  64.3 6.4 collective-permute-done.13
  72.7 5.7 fusion.60
  100.3 5.2 collective-permute-done.20
  109.1 5.7 fusion.58
  136.2 5.2 collective-permute-done.27
  145.0 5.7 fusion.56
  172.3 5.2 collective-permute-done.34
  181.1 5.7 fusion.54
  208.2 5.2 collective-permute-done.41
  217.0 5.7 fusion.52
  253.1 5.7 fusion.50
  280.3 5.2 collective-permute-done.55
  289.1 5.7 fusion.48
  296.9 17.1 %psum.28 = f32[1,2,64]{2,1,0:T(2,128)S(1)} all-reduce(f32[1,2,64]{2,1,0:T(2,128)S(1)} %broadcast_select_fusion.3), channel_id=1, replica_groups=mesh['area'=4,'sub'=8] {'sub'}, use_global_device_ids=true, to_apply=%region_1.2 | all-reduce | flops 128 | bytes 1024 | tf_op jit(solution)/shard_map/psum | solution.py:75
  336.8 6.4 collective-permute-done.64
  345.2 5.7 fusion.46
  372.3 5.2 collective-permute-done.71
  381.1 5.7 fusion.44
  417.2 5.7 fusion.42
  444.3 5.2 collective-permute-done.85
  453.1 5.7 fusion.40
  489.2 5.7 fusion.38
  516.3 5.2 collective-permute-done.99
  525.1 5.7 fusion.36
  561.5 5.7 fusion.34
  588.7 5.2 collective-permute-done.113
  597.4 5.7 fusion.32
  605.2 17.1 %psum.29 = f32[1,2,64]{2,1,0:T(2,128)S(1)} all-reduce(f32[1,2,64]{2,1,0:T(2,128)S(1)} %broadcast_select_fusion.2), channel_id=1, replica_groups=mesh['area'=4,'sub'=8] {'sub'}, use_global_device_ids=true, to_apply=%region_3.4 | all-reduce | flops 128 | bytes 1024 | tf_op jit(solution)/shard_map/psum | solution.py:75
  645.0 6.4 collective-permute-done.122
  653.3 5.7 fusion.30
  679.2 6.4 collective-permute-done.129
  687.6 5.7 fusion.28
  713.9 6.4 collective-permute-done.136
  722.2 5.7 fusion.26
  748.1 6.4 collective-permute-done.143
  756.5 5.7 fusion.24
  782.8 6.4 collective-permute-done.150
  791.1 5.7 fusion.22
  817.1 6.4 collective-permute-done.157
  825.5 5.7 fusion.20
  851.7 6.4 collective-permute-done.164
  860.1 5.7 fusion.18
  886.0 6.4 collective-permute-done.171
  894.4 5.7 fusion.16
  902.2 17.1 %psum.30 = f32[1,2,64]{2,1,0:T(2,128)S(1)} all-reduce(f32[1,2,64]{2,1,0:T(2,128)S(1)} %broadcast_select_fusion.1), channel_id=1, replica_groups=mesh['area'=4,'sub'=8] {'sub'}, use_global_device_ids=true, to_apply=%region_5.6 | all-reduce | flops 128 | bytes 1024 | tf_op jit(solution)/shard_map/psum | solution.py:75
  941.9 6.4 collective-permute-done.180
  950.2 5.7 fusion.14
  976.2 6.4 collective-permute-done.187
  984.6 5.7 fusion.12
  1010.9 6.4 collective-permute-done.194
  1019.2 5.7 fusion.10
  1045.2 6.4 collective-permute-done.201
  1053.5 5.7 fusion.8
  1079.7 6.4 collective-permute-done.208
  1088.0 5.7 fusion.6
  1114.0 6.4 collective-permute-done.215
  1122.4 5.7 fusion.4
  1148.7 6.4 collective-permute-done.222
  1157.0 5.7 fusion.2
  1182.9 6.4 collective-permute-done.229
  1191.3 5.7 fusion
  1198.4 17.1 %psum.31 = f32[1,2,64]{2,1,0:T(2,128)S(1)} all-reduce(f32[1,2,64]{2,1,0:T(2,128)S(1)} %broadcast_select_fusion), channel_id=1, replica_groups=mesh['area'=4,'sub'=8] {'sub'}, use_global_device_ids=true, to_apply=%region_7.8 | all-reduce | flops 128 | bytes 1024 | tf_op jit(solution)/shard_map/psum | solution.py:75
  (1053 shorter events, 797.1 us)
Async XLA Ops:
  0.6 16.4 %collective-permute-start = (f32[1,4096]{1,0:T(1,128)}, f32[1,4096]{1,0:T(1,128)S(1)}, u32[]{:S(2)}, u32[]{:S(2)}) collective-permute-start(f32[1,4096]{1,0:T(1,128)} %param.13), channel_id=1, source_target_pairs={{0,1},{1,2},{2,3},{3,4},{4,5},{5,6},{6,7},{7,0},{8,9},{9,10},{10,1... | collective-permute-start | bytes 49160 | tf_op jit(solution)/shard_map/ppermute | solution.py:19
  3.7 13.4 %collective-permute-start.1 = (f32[1,4096]{1,0:T(1,128)}, f32[1,4096]{1,0:T(1,128)S(1)}, u32[]{:S(2)}, u32[]{:S(2)}) collective-permute-start(f32[1,4096]{1,0:T(1,128)} %param.13), channel_id=1, source_target_pairs={{0,7},{1,0},{2,1},{3,2},{4,3},{5,4},{6,5},{7,6},{8,15},{9,8},{10,9... | collective-permute-start | bytes 49160 | tf_op jit(solution)/shard_map/ppermute | solution.py:24
  17.1 6.5 collective-permute-start.2
  45.0 6.5 collective-permute-start.7
  79.2 6.5 collective-permute-start.14
  79.3 7.1 collective-permute-start.15
  86.4 6.9 collective-permute-start.17
  92.2 6.9 collective-permute-start.18
  115.7 7.0 collective-permute-start.22
  151.7 7.0 collective-permute-start.29
  165.1 6.6 collective-permute-start.33
  171.0 6.6 collective-permute-start.34
  187.7 7.0 collective-permute-start.36
  223.7 7.0 collective-permute-start.43
  237.1 6.7 collective-permute-start.47
  242.9 6.6 collective-permute-start.48
  259.8 7.0 collective-permute-start.50
  314.1 9.4 collective-permute-start.58
  316.1 7.4 collective-permute-start.59
  330.0 6.8 collective-permute-start.63
  336.4 6.8 collective-permute-start.64
  351.8 7.0 collective-permute-start.66
  387.7 7.0 collective-permute-start.73
  401.2 6.6 collective-permute-start.77
  407.0 6.6 collective-permute-start.78
  423.8 7.0 collective-permute-start.80
  459.7 7.0 collective-permute-start.87
  473.2 6.7 collective-permute-start.91
  479.0 6.6 collective-permute-start.92
  495.8 7.0 collective-permute-start.94
  531.7 7.0 collective-permute-start.101
  538.2 6.5 collective-permute-start.102
  538.8 6.5 collective-permute-start.103
  545.3 6.8 collective-permute-start.105
  551.1 6.8 collective-permute-start.106
  568.1 7.0 collective-permute-start.108
  622.4 9.4 collective-permute-start.116
  624.5 7.4 collective-permute-start.117
  638.3 6.6 collective-permute-start.121
  644.7 6.6 collective-permute-start.122
  694.1 6.5 collective-permute-start.130
  700.6 6.6 collective-permute-start.132
  700.6 6.6 collective-permute-start.133
  707.2 6.6 collective-permute-start.135
  713.6 6.6 collective-permute-start.136
  776.0 6.8 collective-permute-start.149
  782.4 6.8 collective-permute-start.150
  844.9 6.6 collective-permute-start.162
  845.0 6.8 collective-permute-start.163
  851.5 6.6 collective-permute-start.164
  919.4 9.4 collective-permute-start.174
  921.4 7.4 collective-permute-start.175
  935.3 6.6 collective-permute-start.179
  941.7 6.6 collective-permute-start.180
  956.8 6.5 collective-permute-start.181
  1004.1 6.8 collective-permute-start.193
  1010.5 6.8 collective-permute-start.194
  1073.0 6.6 collective-permute-start.207
  1079.4 6.6 collective-permute-start.208
  1101.0 6.6 collective-permute-start.211
  1101.0 6.6 collective-permute-start.212
  1141.9 6.6 collective-permute-start.220
  1141.9 6.8 collective-permute-start.221
  1148.4 6.6 collective-permute-start.222
  (178 other events, 1509.0 us)
